TPU v7x, 32 devices: a whole 2x2x4 slice. The times are simulated.
32 devices in a mesh: ctx: 16 (over z, y, x), head: 2 (over core).
Axes of the slice: x: 2, y: 2, z: 4, core: 2. Of those that a mesh axis runs over, the one named last changes fastest.
Arguments:
- activations: bfloat16 [7168, 4096], P('ctx'), may hold values from -150 to 150
- query_weight: bfloat16 [4096, 2048], P('ctx', 'head'), may hold values from -0.09375 to 0.09375
- keyval_weight: bfloat16 [4096, 2, 2048], P('ctx', None, 'head'), may hold values from -0.09375 to 0.09375
- out_weight: bfloat16 [2048, 4096], P('head', 'ctx'), may hold values from -0.125 to 0.125
- norm_gain: float32 [4096], replicated, may hold values from 0.1 to 1.9
- vocab_weight: bfloat16 [63488, 4096], P(('ctx', 'head')), may hold values from -15 to 15
- mask_positions: int32 [16, 16], P('ctx'), may hold values from 0 to 447, as said below
- mask_count: int32 [16], P('ctx'), may hold values from 1 to 16, as said below
- targets: int32 [16, 16], P('ctx'), may hold values from 0 to 63487
Outputs:
- loss: float32 [16, 16], P('ctx')
Inputs may be any that keep to these rules, and one draw needn't show every extreme that they name: `mask_positions`: the 16 entries of a row are distinct; the first mask_count[c] of row c are the masked positions of block c, the others unused. `mask_count`: some block has all 16 slots used.
All inputs are finite; a program needn't handle non-finite values.
Results may differ from a plain program's by a relative error of at most 0.0098.
Values may be sent and summed in bfloat16 or wider, within the bound.
No kernel may reach another device: no remote copies, remote signals or barrier semaphores. Data moves between devices by JAX's collectives and lax.ppermute only.
A program may use at most 128 MiB of HBM per device.

v0:
```python
import jax
import jax.numpy as jnp
from jax import lax
from jax.sharding import PartitionSpec as P

HDIM = 128


def shards(
    activations,
    query_weight,
    keyval_weight,
    out_weight,
    norm_gain,
    vocab_weight,
    mask_positions,
    mask_count,
    targets,
):
    ctx_count = lax.axis_size("ctx")
    block_len = activations.shape[0]
    slot_count = mask_positions.shape[1]
    total_rows = ctx_count * slot_count
    head_columns = query_weight.shape[1]
    heads_here = head_columns // HDIM
    feature_cols = activations
    keyval = jnp.einsum(
        "td,djc->tjc",
        feature_cols,
        lax.all_gather(keyval_weight, "ctx", axis=0, tiled=True),
        preferred_element_type=jnp.float32,
    ).astype(jnp.bfloat16)
    key_heads = keyval[:, 0].reshape(block_len, heads_here, HDIM)
    value_heads = keyval[:, 1].reshape(block_len, heads_here, HDIM)
    rows_here = jnp.take(activations, mask_positions[0], axis=0)
    feature_cols = rows_here
    own_queries = jnp.dot(
        feature_cols,
        lax.all_gather(query_weight, "ctx", axis=0, tiled=True),
        preferred_element_type=jnp.float32,
    ).astype(jnp.bfloat16)
    queries = lax.all_gather(own_queries, "ctx", axis=0, tiled=True)
    query_heads = queries.reshape(total_rows, heads_here, HDIM)
    scores = jnp.einsum(
        "rhc,thc->hrt", query_heads, key_heads, preferred_element_type=jnp.float32
    ) * HDIM ** (-0.5)
    highest = lax.pmax(jnp.max(scores, axis=2), "ctx")
    exponent = jnp.exp(scores - highest[:, :, None])
    weights = exponent.astype(jnp.bfloat16)
    numerator = jnp.einsum(
        "hrt,thc->rhc", weights, value_heads, preferred_element_type=jnp.float32
    ).reshape(total_rows, head_columns)
    denominator = jnp.sum(exponent, axis=2).T
    numerator, denominator = (
        lax.psum_scatter(numerator, "ctx", scatter_dimension=0, tiled=True),
        lax.psum_scatter(denominator, "ctx", scatter_dimension=0, tiled=True),
    )
    attended = (
        (numerator.reshape(slot_count, heads_here, HDIM) / denominator[:, :, None])
        .reshape(slot_count, head_columns)
        .astype(jnp.bfloat16)
    )
    branch_part = jnp.dot(
        attended,
        lax.all_gather(out_weight, "ctx", axis=1, tiled=True),
        preferred_element_type=jnp.float32,
    )
    wanted = lax.all_gather(targets, "ctx", axis=0, tiled=True)
    branch = lax.psum_scatter(branch_part, "head", scatter_dimension=0, tiled=True)
    meansquare = jnp.mean(branch * branch, axis=1, keepdims=True)
    hidden = (branch * lax.rsqrt(meansquare + 1e-06) * norm_gain).astype(jnp.bfloat16)
    gathered = lax.all_gather(hidden, ("ctx", "head"), axis=0, tiled=True)
    logits = lax.dot_general(
        gathered, vocab_weight, (((1,), (1,)), ((), ())), preferred_element_type=jnp.float32
    )
    vocab_start = lax.axis_index(("ctx", "head")) * vocab_weight.shape[0]
    vocab_ids = vocab_start + jnp.arange(vocab_weight.shape[0], dtype=jnp.int32)
    wanted_rows = wanted.reshape(total_rows)
    largest = lax.pmax(jnp.max(logits, axis=1), ("ctx", "head"))
    expsum = jnp.sum(jnp.exp(logits - largest[:, None]), axis=1)
    picked = jnp.sum(jnp.where(vocab_ids[None, :] == wanted_rows[:, None], logits, 0.0), axis=1)
    expsum, picked = lax.psum((expsum, picked), ("ctx", "head"))
    losses = (largest + jnp.log(expsum) - picked).reshape(ctx_count, slot_count)
    block_losses = lax.dynamic_slice_in_dim(losses, lax.axis_index("ctx"), 1, 0)[0]
    active = jnp.arange(slot_count, dtype=jnp.int32) < mask_count[0]
    return jnp.where(active, block_losses, jnp.zeros_like(block_losses))[None, :]


def solution(mesh):
    in_specs = (
        P("ctx", None),
        P("ctx", "head"),
        P("ctx", None, "head"),
        P("head", "ctx"),
        P(),
        P(("ctx", "head"), None),
        P("ctx", None),
        P("ctx"),
        P("ctx", None),
    )
    out_specs = P("ctx", None)
    return jax.shard_map(shards, mesh=mesh, in_specs=in_specs, out_specs=out_specs, check_vma=False)
```

profile of v0, /device:TPU:0, one launch (start us, length us, event | category | flops | bytes accessed | tf_op | source)
XLA Modules:
  0.0 831.2 jit_solution(3566141470585280756)
XLA Ops:
  6.5 0.7 all-gather.8.cloned.1.call-update
  7.3 0.0 all-gather.6.cloned.1.call-start
  7.3 2.6 copy.14
  9.9 0.0 all-gather.6.cloned.1.call-update
  9.9 0.0 reduce-scatter.12.cloned.1.call-start
  10.0 3.3 gather_fusion
  13.3 112.4 %all-gather.8.cloned.1.call-done = bf16[4096,1024]{1,0:T(8,128)(2,1)} async-done(((bf16[256,1024]{1,0:T(8,128)(2,1)}), bf16[4096,1024]{1,0:T(8,128)(2,1)}) %all-gather.8.cloned.1.call-update) | async-done | bytes 8388624 | tf_op jit(solution)/shard_map/all_gather | solution.py:39
  125.7 4.6 convolution_convert_fusion
  130.3 44.7 %all_gather.20 = bf16[256,1024]{1,0:T(8,128)(2,1)S(1)} all-gather(bf16[16,1024]{1,0:T(8,128)(2,1)S(1)} %convolution_convert_fusion), channel_id=1, replica_groups=mesh['ctx'=16,'head'=2] {'ctx'}, dimensions={0}, use_global_device_ids=true | all-gather | bytes 557056 | tf_op jit(solution)/shard_map/all_gather | solution.py:42
  175.0 147.0 %all-gather.6.cloned.1.call-done = bf16[4096,2,1024]{2,0,1:T(8,128)(2,1)} async-done(((bf16[256,2,1024]{2,0,1:T(8,128)(2,1)}), bf16[4096,2,1024]{2,0,1:T(8,128)(2,1)}) %all-gather.6.cloned.1.call-update) | async-done | bytes 16777232 | tf_op jit(solution)/shard_map/all_gather | solution.py:30
  322.0 12.6 %fusion.8 = bf16[448,2,1024]{2,0,1:T(8,128)(2,1)S(1)} fusion(bf16[4096,2,1024]{2,0,1:T(8,128)(2,1)} %all-gather.6.cloned.1.call-done, bf16[448,4096]{1,0:T(8,128)(2,1)} %param.9), kind=kOutput, calls=%fused_computation.12 | convolution fusion | flops 7517110272 | bytes 22282240 | tf_op jit(solution)/shard_map/td,djc->tjc/dot_general | solution.py:27
  334.5 0.1 slice_bitcast_fusion.1
  334.7 0.2 copy.24
  334.9 2.4 multiply_reduce_fusion
  337.4 39.4 %pmax.14 = f32[8,256]{1,0:T(8,128)S(1)} all-reduce(f32[8,256]{1,0:T(8,128)S(1)} %get-tuple-element.11), channel_id=1, replica_groups=mesh['ctx'=16,'head'=2] {'ctx'}, use_global_device_ids=true, to_apply=%region_1.2 | all-reduce | flops 2048 | bytes 16384 | tf_op jit(solution)/shard_map/pmax | solution.py:47
  376.7 0.2 copy.23
  376.9 2.7 fusion.2
  379.6 0.8 copy.20
  380.4 0.0 reduce-scatter.10.cloned.1.call-start
  380.5 2.9 fusion.4
  383.4 1.4 copy.18
  384.8 0.0 reduce-scatter.10.cloned.1.call-update
  384.8 0.0 all-gather.10.cloned.1.call-start
  384.8 0.5 all-gather.10.cloned.1.call-update
  385.4 0.0 reduce-scatter.8.cloned.1.call-start
  385.4 66.8 %reduce-scatter.12.cloned.1.call-done = f32[16,8]{1,0:T(8,128)} async-done(((f32[256,8]{1,0:T(8,128)}), f32[16,8]{1,0:T(8,128)}) %reduce-scatter.12.cloned.1.call-update) | async-done | bytes 528
  452.2 0.8 copy.21
  453.0 75.5 %reduce-scatter.10.cloned.1.call-done = f32[16,1024]{1,0:T(8,128)} async-done(((f32[256,1024]{1,0:T(8,128)}), f32[16,1024]{1,0:T(8,128)}) %reduce-scatter.10.cloned.1.call-update) | async-done | bytes 65552
  528.5 1.0 copy.19
  529.5 0.1 fusion.16
  529.6 133.2 %all-gather.10.cloned.1.call-done = bf16[1024,4096]{1,0:T(8,128)(2,1)} async-done(((bf16[1024,256]{1,0:T(8,128)(2,1)}), bf16[1024,4096]{1,0:T(8,128)(2,1)}) %all-gather.10.cloned.1.call-update) | async-done | bytes 8388624 | tf_op jit(solution)/shard_map/all_gather | solution.py:65
  662.8 5.3 fusion.24
  668.1 0.0 reduce-scatter.8.cloned.1.call-update
  668.2 0.0 all-gather.12.cloned.1.call-start
  668.2 6.0 reduce-scatter.8.cloned.1.call-done
  674.2 1.0 multiply_reduce_fusion.1
  675.2 1.6 multiply_convert_fusion
  676.9 40.8 %all-gather = s32[16,1,16]{2,1,0:T(1,128)S(1)} all-gather(s32[1,1,16]{2,1,0:T(1,128)S(1)} %bitcast.53), channel_id=1, replica_groups=mesh['ctx'=16,'head'=2] {'ctx'}, dimensions={0}, use_global_device_ids=true | all-gather | bytes 1088 | tf_op jit(solution)/shard_map/all_gather | solution.py:68
  717.7 0.5 broadcast.82
  718.2 0.7 reduce.3
  718.9 0.1 eq.16
  719.6 15.4 %all-gather.12.cloned.1.call-done = bf16[256,4096]{1,0:T(8,128)(2,1)} async-done(((bf16[8,4096]{1,0:T(8,128)(2,1)}), bf16[256,4096]{1,0:T(8,128)(2,1)}) %all-gather.12.cloned.1.call-update) | async-done | bytes 2097168 | tf_op jit(solution)/shard_map/all_gather | solution.py:72
  735.0 8.6 %fusion.23 = (f32[256]{0:T(256)S(1)}, f32[256,1984]{0,1:T(8,128)S(1)}) fusion(bf16[256,4096]{1,0:T(8,128)(2,1)} %all-gather.12.cloned.1.call-done, bf16[1984,4096]{1,0:T(8,128)(2,1)} %param.14), kind=kOutput, calls=%fused_computation.39 | convolution fusion | flops 4161257216 | bytes 20382720 | tf_op jit(solution)/shard_map/dot_general | solution.py:73
  743.6 38.7 %pmax.15 = f32[256]{0:T(256)S(1)} all-reduce(f32[256]{0:T(256)S(1)} %get-tuple-element.13), channel_id=1, replica_groups=mesh['ctx'=16,'head'=2] {'ctx','head'}, use_global_device_ids=true, to_apply=%region_8.9 | all-reduce | flops 256 | bytes 2048 | tf_op jit(solution)/shard_map/pmax | solution.py:79
  782.3 0.9 exponential_reduce_fusion
  783.2 40.5 %all-reduce = (f32[256]{0:T(256)S(1)}, f32[256]{0:T(256)S(1)}) all-reduce(f32[256]{0:T(256)S(1)} %get-tuple-element.6, f32[256]{0:T(256)S(1)} %get-tuple-element.5), channel_id=1, replica_groups=mesh['ctx'=16,'head'=2] {'ctx','head'}, use_global_device_ids=true, to_apply=%region_12.13 | all-reduce | flops 512 | bytes 4096 | tf_op jit(solution)/shard_map/psum | solution.py:82
  823.8 0.1 reshape.72
  823.9 0.5 compare_select_fusion.2
  (15 shorter events, 0.1 us)
Async XLA Ops:
  6.5 3.4 copy-start.2
  6.5 119.2 %all-gather.8.cloned.1.call-start = ((), (), s32[]{:S(2)}) async-start(), calls=%async_computation.4 | async-start | bytes 8912896 | tf_op jit(solution)/shard_map/all_gather | solution.py:39
  7.3 314.7 %all-gather.6.cloned.1.call-start = ((), (), s32[]{:S(2)}) async-start(), calls=%async_computation.3 | async-start | bytes 17825792 | tf_op jit(solution)/shard_map/all_gather | solution.py:30
  9.9 442.4 %reduce-scatter.12.cloned.1.call-start = ((), (), s32[]{:S(2)}) async-start(), calls=%async_computation.9 | async-start | bytes 139264
  380.4 148.1 %reduce-scatter.10.cloned.1.call-start = ((), (), s32[]{:S(2)}) async-start(), calls=%async_computation.8 | async-start | bytes 1114112
  384.8 278.0 %all-gather.10.cloned.1.call-start = ((), (), s32[]{:S(2)}) async-start(), calls=%async_computation.5 | async-start | bytes 8912896 | tf_op jit(solution)/shard_map/all_gather | solution.py:65
  385.4 288.8 %reduce-scatter.8.cloned.1.call-start = ((), (), s32[]{:S(2)}) async-start(), calls=%async_computation.6 | async-start | bytes 393216 | tf_op jit(solution)/shard_map/reduce_scatter | solution.py:69
  529.6 145.6 %copy-start = (f32[4096]{0:T(1024)S(1)}, f32[4096]{0:T(1024)}, u32[]{:S(2)}) copy-start(f32[4096]{0:T(1024)} %param.13) | copy-start | bytes 49156
  529.6 147.3 %copy-start.1 = (s32[1,16]{1,0:T(1,128)S(1)}, s32[1,16]{1,0:T(1,128)}, u32[]{:S(2)}) copy-start(s32[1,16]{1,0:T(1,128)} %param.17) | copy-start | bytes 196
  668.2 66.9 %all-gather.12.cloned.1.call-start = ((), (), s32[]{:S(2)}) async-start(), calls=%async_computation.7 | async-start | bytes 2162688 | tf_op jit(solution)/shard_map/all_gather | solution.py:72
Sparse Core Ops, SparseCore 0:
  10.1 115.5 all-gather.7
  128.5 193.4 all-gather.5
  380.5 71.6 reduce-scatter.11
  454.5 74.0 reduce-scatter.9
  531.1 131.7 all-gather.9
  668.3 5.8 reduce-scatter.7
  677.4 57.5 all-gather.11
where the time goes:
time: 832 us; the launch traced here: 831 us
  waiting for transfers between devices  558 us (67%)
  blocking collectives  204 us (25%)
  matrix products  36.4 us (4%)
  between operations  14.3 us (2%)
  local copies, waits for them, and re-layouts  11.1 us (1%)
    all_gather x1, waiting for transfers between devices, shards(): lax.all_gather(keyval_weight, 'ctx', axis=0, tiled=True)  147 us
    unnamed x9, waiting for transfers between devices  144 us
    all_gather x1, waiting for transfers between devices, shards(): lax.all_gather(out_weight, 'ctx', axis=1, tiled=True)  133 us
    all_gather x1, waiting for transfers between devices, shards(): lax.all_gather(query_weight, 'ctx', axis=0, tiled=True)  112 us
    all_gather x1, blocking collectives, shards(): queries = lax.all_gather(own_queries, 'ctx', axis=0, tiled=True)  44.7 us
    all_gather x1, blocking collectives, shards(): wanted = lax.all_gather(targets, 'ctx', axis=0, tiled=True)  40.8 us
    psum x1, blocking collectives, shards(): expsum, picked = lax.psum((expsum, picked), ('ctx', 'head'))  40.5 us
    pmax x1, blocking collectives, shards(): highest = lax.pmax(jnp.max(scores, axis=2), 'ctx')  39.4 us
  transfers between devices with their start and end apart: 7, of which 7 were waited for; matrix products, arithmetic and copies ran while one was open for 2% of the time, Pallas kernels for 0%

commit v1 on v0

--- a/solution.py
+++ b/solution.py
@@ -4,6 +4,11 @@
 from jax.sharding import PartitionSpec as P
 
 HDIM = 128
+
+
+def place_targets_on(mat, which_axis, row_axis):
+    f_next = lax.psum(mat, which_axis)
+    return lax.psum(f_next, row_axis)
 
 
 def shards(
@@ -79,7 +84,7 @@
     largest = lax.pmax(jnp.max(logits, axis=1), ("ctx", "head"))
     expsum = jnp.sum(jnp.exp(logits - largest[:, None]), axis=1)
     picked = jnp.sum(jnp.where(vocab_ids[None, :] == wanted_rows[:, None], logits, 0.0), axis=1)
-    expsum, picked = lax.psum((expsum, picked), ("ctx", "head"))
+    expsum, picked = place_targets_on((expsum, picked), "head", "ctx")
     losses = (largest + jnp.log(expsum) - picked).reshape(ctx_count, slot_count)
     block_losses = lax.dynamic_slice_in_dim(losses, lax.axis_index("ctx"), 1, 0)[0]
     active = jnp.arange(slot_count, dtype=jnp.int32) < mask_count[0]

time: 832 us -> 834 us (level)
    psum x1 -> x2, blocking collectives: 40.5 us -> 43 us  [the longest x1 40.5 us: place_targets_on(): return lax.psum(f_next, row_axis)]
where the time goes in v1:
time: 834 us
  waiting for transfers between devices  558 us (67%)
  blocking collectives  207 us (25%)
  matrix products  36.4 us (4%)
  between operations  14.3 us (2%)
  local copies, waits for them, and re-layouts  11.1 us (1%)
    all_gather x1, waiting for transfers between devices, shards(): lax.all_gather(keyval_weight, 'ctx', axis=0, tiled=True)  147 us
    unnamed x9, waiting for transfers between devices  144 us
    all_gather x1, waiting for transfers between devices, shards(): lax.all_gather(out_weight, 'ctx', axis=1, tiled=True)  133 us
    all_gather x1, waiting for transfers between devices, shards(): lax.all_gather(query_weight, 'ctx', axis=0, tiled=True)  112 us
    all_gather x1, blocking collectives, shards(): queries = lax.all_gather(own_queries, 'ctx', axis=0, tiled=True)  44.7 us
    all_gather x1, blocking collectives, shards(): wanted = lax.all_gather(targets, 'ctx', axis=0, tiled=True)  40.8 us
    psum x1, blocking collectives, place_targets_on(): return lax.psum(f_next, row_axis)  40.5 us
    pmax x1, blocking collectives, shards(): highest = lax.pmax(jnp.max(scores, axis=2), 'ctx')  39.4 us
  transfers between devices with their start and end apart: 7, of which 7 were waited for; matrix products, arithmetic and copies ran while one was open for 2% of the time, Pallas kernels for 0%

profile of v1, /device:TPU:0, one launch (start us, length us, event | category | flops | bytes accessed | tf_op | source)
XLA Modules:
  0.0 833.7 jit_solution(2480603452913706395)
XLA Ops:
  6.5 0.7 all-gather.8.cloned.1.call-update
  7.3 0.0 all-gather.6.cloned.1.call-start
  7.3 2.6 copy.14
  9.9 0.0 all-gather.6.cloned.1.call-update
  9.9 0.0 reduce-scatter.12.cloned.1.call-start
  10.0 3.3 gather_fusion
  13.3 112.4 %all-gather.8.cloned.1.call-done = bf16[4096,1024]{1,0:T(8,128)(2,1)} async-done(((bf16[256,1024]{1,0:T(8,128)(2,1)}), bf16[4096,1024]{1,0:T(8,128)(2,1)}) %all-gather.8.cloned.1.call-update) | async-done | bytes 8388624 | tf_op jit(solution)/shard_map/all_gather | solution.py:44
  125.7 4.6 convolution_convert_fusion
  130.3 44.7 %all_gather.20 = bf16[256,1024]{1,0:T(8,128)(2,1)S(1)} all-gather(bf16[16,1024]{1,0:T(8,128)(2,1)S(1)} %convolution_convert_fusion), channel_id=1, replica_groups=mesh['ctx'=16,'head'=2] {'ctx'}, dimensions={0}, use_global_device_ids=true | all-gather | bytes 557056 | tf_op jit(solution)/shard_map/all_gather | solution.py:47
  175.0 147.0 %all-gather.6.cloned.1.call-done = bf16[4096,2,1024]{2,0,1:T(8,128)(2,1)} async-done(((bf16[256,2,1024]{2,0,1:T(8,128)(2,1)}), bf16[4096,2,1024]{2,0,1:T(8,128)(2,1)}) %all-gather.6.cloned.1.call-update) | async-done | bytes 16777232 | tf_op jit(solution)/shard_map/all_gather | solution.py:35
  322.0 12.6 %fusion.8 = bf16[448,2,1024]{2,0,1:T(8,128)(2,1)S(1)} fusion(bf16[4096,2,1024]{2,0,1:T(8,128)(2,1)} %all-gather.6.cloned.1.call-done, bf16[448,4096]{1,0:T(8,128)(2,1)} %param.9), kind=kOutput, calls=%fused_computation.12 | convolution fusion | flops 7517110272 | bytes 22282240 | tf_op jit(solution)/shard_map/td,djc->tjc/dot_general | solution.py:32
  334.5 0.1 slice_bitcast_fusion.1
  334.7 0.2 copy.24
  334.9 2.4 multiply_reduce_fusion
  337.4 39.4 %pmax.14 = f32[8,256]{1,0:T(8,128)S(1)} all-reduce(f32[8,256]{1,0:T(8,128)S(1)} %get-tuple-element.13), channel_id=1, replica_groups=mesh['ctx'=16,'head'=2] {'ctx'}, use_global_device_ids=true, to_apply=%region_1.2 | all-reduce | flops 2048 | bytes 16384 | tf_op jit(solution)/shard_map/pmax | solution.py:52
  376.7 0.2 copy.23
  376.9 2.7 fusion.2
  379.6 0.8 copy.20
  380.4 0.0 reduce-scatter.10.cloned.1.call-start
  380.5 2.9 fusion.4
  383.4 1.4 copy.18
  384.8 0.0 reduce-scatter.10.cloned.1.call-update
  384.8 0.0 all-gather.10.cloned.1.call-start
  384.8 0.5 all-gather.10.cloned.1.call-update
  385.4 0.0 reduce-scatter.8.cloned.1.call-start
  385.4 66.8 %reduce-scatter.12.cloned.1.call-done = f32[16,8]{1,0:T(8,128)} async-done(((f32[256,8]{1,0:T(8,128)}), f32[16,8]{1,0:T(8,128)}) %reduce-scatter.12.cloned.1.call-update) | async-done | bytes 528
  452.2 0.8 copy.21
  453.0 75.5 %reduce-scatter.10.cloned.1.call-done = f32[16,1024]{1,0:T(8,128)} async-done(((f32[256,1024]{1,0:T(8,128)}), f32[16,1024]{1,0:T(8,128)}) %reduce-scatter.10.cloned.1.call-update) | async-done | bytes 65552
  528.5 1.0 copy.19
  529.5 0.1 fusion.16
  529.6 133.2 %all-gather.10.cloned.1.call-done = bf16[1024,4096]{1,0:T(8,128)(2,1)} async-done(((bf16[1024,256]{1,0:T(8,128)(2,1)}), bf16[1024,4096]{1,0:T(8,128)(2,1)}) %all-gather.10.cloned.1.call-update) | async-done | bytes 8388624 | tf_op jit(solution)/shard_map/all_gather | solution.py:70
  662.8 5.3 fusion.24
  668.2 0.0 all-gather.12.cloned.1.call-start
  668.2 6.0 reduce-scatter.8.cloned.1.call-done
  674.2 1.0 multiply_reduce_fusion.1
  675.2 1.6 multiply_convert_fusion
  676.9 40.8 %all-gather = s32[16,1,16]{2,1,0:T(1,128)S(1)} all-gather(s32[1,1,16]{2,1,0:T(1,128)S(1)} %bitcast.53), channel_id=1, replica_groups=mesh['ctx'=16,'head'=2] {'ctx'}, dimensions={0}, use_global_device_ids=true | all-gather | bytes 1088 | tf_op jit(solution)/shard_map/all_gather | solution.py:73
  717.7 0.5 broadcast.82
  718.2 0.7 reduce.3
  718.9 0.1 eq.16
  719.6 15.4 %all-gather.12.cloned.1.call-done = bf16[256,4096]{1,0:T(8,128)(2,1)} async-done(((bf16[8,4096]{1,0:T(8,128)(2,1)}), bf16[256,4096]{1,0:T(8,128)(2,1)}) %all-gather.12.cloned.1.call-update) | async-done | bytes 2097168 | tf_op jit(solution)/shard_map/all_gather | solution.py:77
  735.0 8.6 %fusion.23 = (f32[256]{0:T(256)S(1)}, f32[256,1984]{0,1:T(8,128)S(1)}) fusion(bf16[256,4096]{1,0:T(8,128)(2,1)} %all-gather.12.cloned.1.call-done, bf16[1984,4096]{1,0:T(8,128)(2,1)} %param.14), kind=kOutput, calls=%fused_computation.39 | convolution fusion | flops 4161257216 | bytes 20382720 | tf_op jit(solution)/shard_map/dot_general | solution.py:78
  743.6 38.7 %pmax.15 = f32[256]{0:T(256)S(1)} all-reduce(f32[256]{0:T(256)S(1)} %get-tuple-element.15), channel_id=1, replica_groups=mesh['ctx'=16,'head'=2] {'ctx','head'}, use_global_device_ids=true, to_apply=%region_8.9 | all-reduce | flops 256 | bytes 2048 | tf_op jit(solution)/shard_map/pmax | solution.py:84
  782.3 0.9 exponential_reduce_fusion
  783.2 2.5 all-reduce.1
  785.7 40.5 %all-reduce = (f32[256]{0:T(256)S(1)}, f32[256]{0:T(256)S(1)}) all-reduce(f32[256]{0:T(256)S(1)} %get-tuple-element.9, f32[256]{0:T(256)S(1)} %get-tuple-element.10), channel_id=1, replica_groups=mesh['ctx'=16,'head'=2] {'ctx'}, use_global_device_ids=true, to_apply=%region_14.15 | all-reduce | flops 512 | bytes 4096 | tf_op jit(solution)/shard_map/psum | solution.py:11
  826.2 0.1 reshape.72
  826.3 0.5 compare_select_fusion.2
  (16 shorter events, 0.1 us)
Async XLA Ops:
  6.5 3.4 copy-start.2
  6.5 119.2 %all-gather.8.cloned.1.call-start = ((), (), s32[]{:S(2)}) async-start(), calls=%async_computation.4 | async-start | bytes 8912896 | tf_op jit(solution)/shard_map/all_gather | solution.py:44
  7.3 314.7 %all-gather.6.cloned.1.call-start = ((), (), s32[]{:S(2)}) async-start(), calls=%async_computation.3 | async-start | bytes 17825792 | tf_op jit(solution)/shard_map/all_gather | solution.py:35
  9.9 442.4 %reduce-scatter.12.cloned.1.call-start = ((), (), s32[]{:S(2)}) async-start(), calls=%async_computation.9 | async-start | bytes 139264
  380.4 148.1 %reduce-scatter.10.cloned.1.call-start = ((), (), s32[]{:S(2)}) async-start(), calls=%async_computation.8 | async-start | bytes 1114112
  384.8 278.0 %all-gather.10.cloned.1.call-start = ((), (), s32[]{:S(2)}) async-start(), calls=%async_computation.5 | async-start | bytes 8912896 | tf_op jit(solution)/shard_map/all_gather | solution.py:70
  385.4 288.8 %reduce-scatter.8.cloned.1.call-start = ((), (), s32[]{:S(2)}) async-start(), calls=%async_computation.6 | async-start | bytes 393216 | tf_op jit(solution)/shard_map/reduce_scatter | solution.py:74
  529.6 145.6 %copy-start = (f32[4096]{0:T(1024)S(1)}, f32[4096]{0:T(1024)}, u32[]{:S(2)}) copy-start(f32[4096]{0:T(1024)} %param.13) | copy-start | bytes 49156
  529.6 147.3 %copy-start.1 = (s32[1,16]{1,0:T(1,128)S(1)}, s32[1,16]{1,0:T(1,128)}, u32[]{:S(2)}) copy-start(s32[1,16]{1,0:T(1,128)} %param.17) | copy-start | bytes 196
  668.2 66.9 %all-gather.12.cloned.1.call-start = ((), (), s32[]{:S(2)}) async-start(), calls=%async_computation.7 | async-start | bytes 2162688 | tf_op jit(solution)/shard_map/all_gather | solution.py:77
Sparse Core Ops, SparseCore 0:
  10.1 115.5 all-gather.7
  128.5 193.4 all-gather.5
  380.5 71.6 reduce-scatter.11
  454.5 74.0 reduce-scatter.9
  531.1 131.7 all-gather.9
  668.3 5.8 reduce-scatter.7
  677.4 57.5 all-gather.11
